TPU v7x, 128 devices: a whole 4x4x4 slice. The times are simulated.
128 devices in a mesh: dp: 32 (over y, z_lo, x), tensor: 4 (over z_hi, core).
Axes of the slice: x: 4, y: 4, z: 4 (z_hi: 2, z_lo: 2; z = z_hi * 2 + z_lo), core: 2. Of those that a mesh axis runs over, the one named last changes fastest.
Arguments:
- tokens: bfloat16 [32768, 4096], P('dp'), may hold values from -6 to 6
- grad_out: bfloat16 [32768, 2048], P('dp', 'tensor'), may hold values from -12 to 12
- w_query: bfloat16 [4096, 2048], P('dp', 'tensor'), may hold values from -2 to 2
- w_key: bfloat16 [4096, 512], P('dp', 'tensor'), may hold values from -2 to 2
- value_matrix: bfloat16 [4096, 512], P('dp', 'tensor'), may hold values from -0.09375 to 0.09375
Outputs:
- grad_tokens: bfloat16 [32768, 4096], P('dp', 'tensor')
- grad_query: bfloat16 [4096, 2048], P('dp', 'tensor')
- grad_key: bfloat16 [4096, 512], P('dp', 'tensor')
- grad_value: bfloat16 [4096, 512], P('dp', 'tensor')
All inputs are finite; a program needn't handle non-finite values.
Results may differ from a plain program's by a relative error of at most 0.03.
The roundings to bfloat16 on the way count: a program that leaves them out, or rounds other values in their place, can miss the bound.
Values may be sent and summed in bfloat16 or wider, within the bound.
No kernel may reach another device: no remote copies, remote signals or barrier semaphores. Data moves between devices by JAX's collectives and lax.ppermute only.
A program may use at most 192 MiB of HBM per device.

v0:
```python
import jax
import jax.numpy as jnp
from jax import lax
from jax.sharding import PartitionSpec as P

MODEL_WIDTH = 4096
HEAD_SIZE = 128


rope_base = 500000.0


def position_tables(length, head_dim):
    half_dim = head_dim // 2
    positions = jnp.arange(length, dtype=jnp.float32)
    inverse = jnp.power(
        jnp.float32(rope_base), -2.0 * jnp.arange(half_dim, dtype=jnp.float32) / head_dim
    )
    angles = positions[:, None] * inverse[None, :]
    cosine = jnp.concatenate([jnp.cos(angles), jnp.cos(angles)], axis=-1)[:, None, :]
    sine_table = jnp.concatenate([jnp.sin(angles), jnp.sin(angles)], axis=-1)[:, None, :]
    return (cosine, sine_table)


def half_turn(values):
    lower, upper = jnp.split(values, 2, axis=-1)
    return jnp.concatenate([-upper, lower], axis=-1)


def rotate_forward(values, cosine, sine_table):
    return values * cosine + half_turn(values) * sine_table


def rotate_back(grads, cosine, sine_table):
    return grads * cosine - half_turn(grads * sine_table)


def attention_backward(unrotated_query, unrotated_key, projected_value, upstream_flat, kv_heads):
    length = unrotated_query.shape[0]
    heads = unrotated_query.shape[1] // HEAD_SIZE
    group_size = heads // kv_heads
    cosine, sine_table = position_tables(length, HEAD_SIZE)
    query = rotate_forward(
        unrotated_query.reshape(length, heads, HEAD_SIZE), cosine, sine_table
    ).astype(jnp.bfloat16)
    key = rotate_forward(
        unrotated_key.reshape(length, kv_heads, HEAD_SIZE), cosine, sine_table
    ).astype(jnp.bfloat16)
    value = projected_value.reshape(length, kv_heads, HEAD_SIZE).astype(jnp.bfloat16)
    query_grouped = query.reshape(length, kv_heads, group_size, HEAD_SIZE)
    upstream = upstream_flat.reshape(length, kv_heads, group_size, HEAD_SIZE)
    scale = 1.0 / jnp.sqrt(jnp.float32(HEAD_SIZE))
    scores = (
        jnp.einsum("ikgd,jkd->kgij", query_grouped, key, preferred_element_type=jnp.float32) * scale
    )
    positions = jnp.arange(length, dtype=jnp.int32)
    causal = positions[:, None] >= positions[None, :]
    scores = jnp.where(causal, scores, -jnp.inf)
    row_max = jnp.max(scores, axis=-1, keepdims=True)
    weights = jnp.exp(scores - row_max)
    weights = weights / jnp.sum(weights, axis=-1, keepdims=True)
    weights_b = weights.astype(jnp.bfloat16)
    dprob = jnp.einsum("ikgd,jkd->kgij", upstream, value, preferred_element_type=jnp.float32)
    rowdot = jnp.sum(weights * dprob, axis=-1, keepdims=True)
    dscore = (weights * (dprob - rowdot) * scale).astype(jnp.bfloat16)
    dquery = jnp.einsum("kgij,jkd->ikgd", dscore, key, preferred_element_type=jnp.float32).reshape(
        length, heads, HEAD_SIZE
    )
    dkey = jnp.einsum("kgij,ikgd->jkd", dscore, query_grouped, preferred_element_type=jnp.float32)
    dvalue = jnp.einsum("kgij,ikgd->jkd", weights_b, upstream, preferred_element_type=jnp.float32)
    query_gradient = (
        rotate_back(dquery, cosine, sine_table)
        .astype(jnp.bfloat16)
        .reshape(length, heads * HEAD_SIZE)
    )
    key_gradient = (
        rotate_back(dkey, cosine, sine_table)
        .astype(jnp.bfloat16)
        .reshape(length, kv_heads * HEAD_SIZE)
    )
    value_gradient = dvalue.astype(jnp.bfloat16).reshape(length, kv_heads * HEAD_SIZE)
    return (query_gradient, key_gradient, value_gradient)


def contract_cols(grads, weight_rows):
    return lax.dot_general(
        grads, weight_rows, (((1,), (1,)), ((), ())), preferred_element_type=jnp.float32
    )


def body(tokens, grad_out, w_query, w_key, value_matrix):
    query_cols = w_query.shape[1]
    key_value_columns = w_key.shape[1]
    kv_dev = key_value_columns // HEAD_SIZE
    pieces = (
        lax.all_gather(w_query, "dp", axis=0, tiled=True),
        lax.all_gather(w_key, "dp", axis=0, tiled=True),
        lax.all_gather(value_matrix, "dp", axis=0, tiled=True),
    )
    unrotated_query, unrotated_key, projected_value = tuple(
        (jnp.dot(tokens, piece, preferred_element_type=jnp.float32) for piece in pieces)
    )
    query_gradient, key_gradient, value_gradient = attention_backward(
        unrotated_query, unrotated_key, projected_value, grad_out, kv_dev
    )
    combined = jnp.concatenate([query_gradient, key_gradient, value_gradient], axis=1)
    pieces = lax.all_gather((w_query, w_key, value_matrix), "dp", axis=0, tiled=True)
    partial_sum = (
        contract_cols(query_gradient, pieces[0])
        + contract_cols(key_gradient, pieces[1])
        + contract_cols(value_gradient, pieces[2])
    )
    summed_all = lax.psum(partial_sum.astype(jnp.bfloat16), "tensor").astype(jnp.float32)
    share_width = MODEL_WIDTH // lax.axis_size("tensor")
    grad_tokens = lax.dynamic_slice_in_dim(
        summed_all, lax.axis_index("tensor") * share_width, share_width, 1
    )
    grads_all = lax.psum_scatter(
        lax.dot_general(
            tokens, combined, (((0,), (0,)), ((), ())), preferred_element_type=jnp.float32
        ).astype(jnp.bfloat16),
        "dp",
        scatter_dimension=0,
        tiled=True,
    ).astype(jnp.float32)
    grad_query = grads_all[:, :query_cols].astype(jnp.bfloat16)
    grad_key = grads_all[:, query_cols : query_cols + key_value_columns].astype(jnp.bfloat16)
    grad_value = grads_all[:, query_cols + key_value_columns :].astype(jnp.bfloat16)
    return (grad_tokens.astype(jnp.bfloat16), grad_query, grad_key, grad_value)


def solution(mesh):
    in_specs = (
        P("dp", None),
        P("dp", "tensor"),
        P("dp", "tensor"),
        P("dp", "tensor"),
        P("dp", "tensor"),
    )
    out_specs = (P("dp", "tensor"), P("dp", "tensor"), P("dp", "tensor"), P("dp", "tensor"))
    return jax.shard_map(body, mesh=mesh, in_specs=in_specs, out_specs=out_specs, check_vma=False)
```

profile of v0, /device:TPU:0, one launch (start us, length us, event | category | flops | bytes accessed | tf_op | source)
XLA Modules:
  0.0 889.6 jit_solution(15293957988102845399)
XLA Ops:
  7.2 0.0 all-gather.4.cloned.1.call-start
  7.2 0.7 all-gather.4.cloned.1.call-update
  7.9 0.0 all-gather.6.cloned.1.call-start
  7.9 0.7 all-gather.6.cloned.1.call-update
  8.6 0.0 all-gather.8.cloned.1.call-start
  8.7 0.7 all-gather.8.cloned.1.call-update
  9.4 0.0 all-reduce.2.cloned.1.call-start
  9.4 0.3 iota_compare_fusion
  9.8 1.0 fusion.38
  10.8 0.0 copy-start.10
  10.8 2.4 copy.40
  13.1 149.9 %all-gather.4.cloned.1.call-done = bf16[4096,128]{1,0:T(8,128)(2,1)} async-done(((bf16[128,128]{1,0:T(8,128)(2,1)}), bf16[4096,128]{1,0:T(8,128)(2,1)}) %all-gather.4.cloned.1.call-update) | async-done | bytes 1048592 | tf_op jit(solution)/shard_map/all_gather | solution.py:97
  163.1 6.5 fusion.43
  169.6 1.2 pad_maximum_fusion.1
  170.8 151.1 %all-gather.6.cloned.1.call-done = bf16[4096,512]{1,0:T(8,128)(2,1)} async-done(((bf16[128,512]{1,0:T(8,128)(2,1)}), bf16[4096,512]{1,0:T(8,128)(2,1)}) %all-gather.6.cloned.1.call-update) | async-done | bytes 4194320 | tf_op jit(solution)/shard_map/all_gather | solution.py:96
  321.9 8.3 fusion.44
  330.2 0.2 slice_negate_fusion.1
  330.4 0.2 maximum_multiply_fusion
  330.6 0.0 copy-start.1
  330.6 0.6 copy-done.3
  331.2 0.6 fusion.14
  331.8 0.1 copy-done.1
  331.9 3.1 fusion.6
  335.1 3.6 fusion.5
  338.7 2.3 copy-done
  341.0 6.0 fusion.25
  347.0 127.4 %all-gather.8.cloned.1.call-done = bf16[4096,128]{1,0:T(8,128)(2,1)} async-done(((bf16[128,128]{1,0:T(8,128)(2,1)}), bf16[4096,128]{1,0:T(8,128)(2,1)}) %all-gather.8.cloned.1.call-update) | async-done | bytes 1048592 | tf_op jit(solution)/shard_map/all_gather | solution.py:98
  474.4 18.2 %fusion = (f32[4,1024]{1,0:T(4,128)S(1)}, f32[1024,1024,4]{1,0,2:T(8,128)}) fusion(f32[4,1024]{1,0:T(4,128)S(1)} %fusion.5, f32[4,1024]{1,0:T(4,128)S(1)} %get-tuple-element.27, f32[1024,1024,4]{1,0,2:T(8,128)} %copy-done, pred[1024,1024]{0,1:T(8,128)(4,1)S(1)} %iota_compare_fusion, bf16[1024,4,128]{0,2,1:T(8,128)(2,1)} %bitcast.132, ...), kind=kOutput, calls=%fused_computation.3 | convolution fusion | flops 2172776448 | bytes 45137920 | tf_op jit(solution)/shard_map/ikgd,jkd->kgij/dot_general | solution.py:63
  492.7 13.4 %fusion.7 = bf16[4,1024,1024]{1,2,0:T(8,128)(2,1)S(1)} fusion(f32[1024,1024,4]{1,0,2:T(8,128)} %get-tuple-element.30, f32[4,1024]{1,0:T(4,128)S(1)} %get-tuple-element.29, f32[4,1024]{1,0:T(4,128)S(1)} %fusion.5, f32[4,1024]{1,0:T(4,128)S(1)} %get-tuple-element.27, f32[1024,1024,4]{1,0,2:T(8,128)} %copy-done, pred[1024,1024]{0,1:T(8,128)(4,1)S(1)} %iota_compare_fusion), kind=kLoop, calls=%fused_computation.12 | loop fusion | flops 33554432 | bytes 43040768 | tf_op jit(solution)/shard_map/reshape.19
  506.1 3.0 bitcast_multiply_fusion.4
  509.1 1.4 bitcast_multiply_fusion.3
  510.5 0.3 slice_negate_fusion
  510.8 0.2 pad_maximum_fusion
  511.0 0.6 fusion.16
  511.7 0.1 fusion.34
  511.8 8.1 fusion.46
  519.9 8.1 fusion.45
  528.0 15.3 %add_convert_fusion = bf16[1024,4096]{1,0:T(8,128)(2,1)} fusion(f32[1024,4096]{1,0:T(8,128)} %fusion.45, f32[1024,4096]{1,0:T(8,128)} %fusion.46, bf16[1024,128]{0,1:T(8,128)(2,1)S(1)} %copy-done.14, bf16[4096,128]{1,0:T(8,128)(2,1)S(1)} %copy-done.13), kind=kOutput, calls=%fused_computation.7 | convolution fusion | flops 1086324736 | bytes 43253760 | tf_op jit(solution)/shard_map/dot_general | solution.py:86
  543.4 0.0 all-reduce.2.cloned.1.call-update
  543.4 0.0 reduce-scatter.4.cloned.1.call-start
  543.4 13.3 %fusion.11 = bf16[4096,768]{0,1:T(8,128)(2,1)} fusion(bf16[1024,4096]{1,0:T(8,128)(2,1)} %param.5, bf16[1024,128]{0,1:T(8,128)(2,1)S(1)} %copy-done.14, bf16[1024,128]{0,1:T(8,128)(2,1)S(1)} %fusion.34, bf16[1024,512]{0,1:T(8,128)(2,1)S(1)} %fusion.16), kind=kOutput, calls=%fused_computation.17 | convolution fusion | flops 6450315264 | bytes 16252928 | tf_op jit(solution)/shard_map/dot_general | solution.py:119
  556.7 8.5 copy.35
  565.2 0.0 reduce-scatter.4.cloned.1.call-update
  565.2 138.8 %all-reduce.2.cloned.1.call-done = bf16[1024,4096]{1,0:T(8,128)(2,1)} async-done(((bf16[1024,4096]{1,0:T(8,128)(2,1)}), bf16[1024,4096]{1,0:T(8,128)(2,1)}) %all-reduce.2.cloned.1.call-update) | async-done | bytes 8388624 | tf_op jit(solution)/shard_map/psum | solution.py:113
  704.0 3.1 convert_convert_fusion
  707.1 173.1 %reduce-scatter.4.cloned.1.call-done = bf16[128,768]{1,0:T(8,128)(2,1)} async-done(((bf16[4096,768]{1,0:T(8,128)(2,1)}), bf16[128,768]{1,0:T(8,128)(2,1)}) %reduce-scatter.4.cloned.1.call-update) | async-done | bytes 196624
  880.1 1.6 slice.15
  881.7 1.4 fusion.42
  (30 shorter events, 0.1 us)
Async XLA Ops:
  7.2 155.9 %all-gather.4.cloned.1.call-start = ((), (), s32[]{:S(2)}) async-start(), calls=%async_computation.1 | async-start | bytes 1081344 | tf_op jit(solution)/shard_map/all_gather | solution.py:97
  7.9 314.0 %all-gather.6.cloned.1.call-start = ((), (), s32[]{:S(2)}) async-start(), calls=%async_computation.2 | async-start | bytes 4325376 | tf_op jit(solution)/shard_map/all_gather | solution.py:96
  8.6 465.8 %all-gather.8.cloned.1.call-start = ((), (), s32[]{:S(2)}) async-start(), calls=%async_computation.3 | async-start | bytes 1081344 | tf_op jit(solution)/shard_map/all_gather | solution.py:98
  9.4 694.6 %all-reduce.2.cloned.1.call-start = ((), (), s32[]{:S(2)}) async-start(), calls=%async_computation.4 | async-start | bytes 16777216 | tf_op jit(solution)/shard_map/psum | solution.py:113
  10.8 158.9 %copy-start.10 = (f32[1024,64]{0,1:T(8,128)}, f32[1024,64]{0,1:T(8,128)S(1)}, u32[]{:S(2)}) copy-start(f32[1024,64]{0,1:T(8,128)S(1)} %get-tuple-element.25) | copy-start | bytes 786436
  321.9 8.5 copy-start.5
  330.2 1.0 copy-start.3
  330.2 1.7 copy-start.8
  330.6 1.3 copy-start.1
  335.0 5.9 copy-start
  335.1 5.9 copy-start.12
  492.6 13.4 %copy-start.2 = (f32[1024,4,128]{0,2,1:T(8,128)S(1)}, f32[1024,4,128]{0,2,1:T(8,128)}, u32[]{:S(2)}) copy-start(f32[1024,4,128]{0,2,1:T(8,128)} %copy-done.1) | copy-start | bytes 6291460
  492.7 13.4 %copy-start.4 = (f32[1024,128]{0,1:T(8,128)S(1)}, f32[1024,128]{0,1:T(8,128)}, u32[]{:S(2)}) copy-start(f32[1024,128]{0,1:T(8,128)} %get-tuple-element.20) | copy-start | bytes 1572868
  506.1 3.0 copy-start.6
  506.1 3.0 copy-start.9
  510.5 1.2 copy-start.11
  510.5 1.3 copy-start.7
  511.8 8.1 copy-start.15
  519.9 8.1 copy-start.13
  519.9 8.1 copy-start.14
  543.4 336.8 %reduce-scatter.4.cloned.1.call-start = ((), (), s32[]{:S(2)}) async-start(), calls=%async_computation.5 | async-start | bytes 6488064
Sparse Core Ops, SparseCore 0:
  9.6 153.3 all-gather.3
  164.7 157.1 all-gather.5
  323.5 150.8 all-gather.7
  543.5 160.4 all-reduce.1
  706.3 173.8 reduce-scatter.3
where the time goes:
time: 890 us
  waiting for transfers between devices  742 us (83%)
  matrix products  91.3 us (10%)
  other arithmetic  24.8 us (3%)
  local copies, waits for them, and re-layouts  16.8 us (2%)
  between operations  14.1 us (2%)
    unnamed x6, waiting for transfers between devices  175 us
    all_gather x1, waiting for transfers between devices, body(): lax.all_gather(w_query, 'dp', axis=0, tiled=True)  151 us
    all_gather x1, waiting for transfers between devices, body(): lax.all_gather(w_key, 'dp', axis=0, tiled=True)  150 us
    psum x1, waiting for transfers between devices, body(): lax.psum(partial_sum.astype(jnp.bfloat16), 'tensor').astype(jnp.float32)  139 us
    all_gather x1, waiting for transfers between devices, body(): lax.all_gather(value_matrix, 'dp', axis=0, tiled=True)  127 us
    dot_general x3, matrix products, contract_cols(): lax.dot_general(grads, weight_rows, (((1,), (1,)), ((), ())), preferred_e...  31.5 us
    dot_general x1, matrix products, attention_backward(): jnp.einsum('ikgd,jkd->kgij', upstream, value, preferred_element_type=jnp....  18.2 us
  transfers between devices with their start and end apart: 5, of which 5 were waited for; matrix products, arithmetic and copies ran while one was open for 7% of the time, Pallas kernels for 0%

commit v1 on v0

--- a/solution.py
+++ b/solution.py
@@ -1,6 +1,7 @@
 import jax
 import jax.numpy as jnp
 from jax import lax
+from jax.sharding import Mesh
 from jax.sharding import PartitionSpec as P
 
 MODEL_WIDTH = 4096
@@ -82,60 +83,56 @@
     return (query_gradient, key_gradient, value_gradient)
 
 
-def contract_cols(grads, weight_rows):
-    return lax.dot_general(
-        grads, weight_rows, (((1,), (1,)), ((), ())), preferred_element_type=jnp.float32
-    )
+DP_AXES = ("y", "zl", "x")
+TP_AXES = ("zh", "c")
+
+
+def gather_rows(block):
+    block = lax.all_gather(block, "x", axis=0, tiled=True)
+    block = lax.all_gather(block, "zl", axis=0, tiled=True)
+    return lax.all_gather(block, "y", axis=0, tiled=True)
+
+
+def scatter_rows(block):
+    block = lax.psum_scatter(block, "y", scatter_dimension=0, tiled=True)
+    block = lax.psum_scatter(block, "zl", scatter_dimension=0, tiled=True)
+    return lax.psum_scatter(block, "x", scatter_dimension=0, tiled=True)
 
 
 def body(tokens, grad_out, w_query, w_key, value_matrix):
     query_cols = w_query.shape[1]
     key_value_columns = w_key.shape[1]
     kv_dev = key_value_columns // HEAD_SIZE
-    pieces = (
-        lax.all_gather(w_query, "dp", axis=0, tiled=True),
-        lax.all_gather(w_key, "dp", axis=0, tiled=True),
-        lax.all_gather(value_matrix, "dp", axis=0, tiled=True),
-    )
-    unrotated_query, unrotated_key, projected_value = tuple(
-        (jnp.dot(tokens, piece, preferred_element_type=jnp.float32) for piece in pieces)
-    )
+    weights_all = gather_rows(jnp.concatenate([w_query, w_key, value_matrix], axis=1))
+    projected = jnp.dot(tokens, weights_all, preferred_element_type=jnp.float32)
+    unrotated_query = projected[:, :query_cols]
+    unrotated_key = projected[:, query_cols : query_cols + key_value_columns]
+    projected_value = projected[:, query_cols + key_value_columns :]
     query_gradient, key_gradient, value_gradient = attention_backward(
         unrotated_query, unrotated_key, projected_value, grad_out, kv_dev
     )
     combined = jnp.concatenate([query_gradient, key_gradient, value_gradient], axis=1)
-    pieces = lax.all_gather((w_query, w_key, value_matrix), "dp", axis=0, tiled=True)
-    partial_sum = (
-        contract_cols(query_gradient, pieces[0])
-        + contract_cols(key_gradient, pieces[1])
-        + contract_cols(value_gradient, pieces[2])
+    partial_sum = lax.dot_general(
+        combined, weights_all, (((1,), (1,)), ((), ())), preferred_element_type=jnp.float32
     )
-    summed_all = lax.psum(partial_sum.astype(jnp.bfloat16), "tensor").astype(jnp.float32)
-    share_width = MODEL_WIDTH // lax.axis_size("tensor")
-    grad_tokens = lax.dynamic_slice_in_dim(
-        summed_all, lax.axis_index("tensor") * share_width, share_width, 1
+    grad_tokens = lax.psum_scatter(
+        partial_sum.astype(jnp.bfloat16), TP_AXES, scatter_dimension=1, tiled=True
     )
-    grads_all = lax.psum_scatter(
+    grads_all = scatter_rows(
         lax.dot_general(
             tokens, combined, (((0,), (0,)), ((), ())), preferred_element_type=jnp.float32
-        ).astype(jnp.bfloat16),
-        "dp",
-        scatter_dimension=0,
-        tiled=True,
-    ).astype(jnp.float32)
-    grad_query = grads_all[:, :query_cols].astype(jnp.bfloat16)
-    grad_key = grads_all[:, query_cols : query_cols + key_value_columns].astype(jnp.bfloat16)
-    grad_value = grads_all[:, query_cols + key_value_columns :].astype(jnp.bfloat16)
-    return (grad_tokens.astype(jnp.bfloat16), grad_query, grad_key, grad_value)
+        ).astype(jnp.bfloat16)
+    )
+    grad_query = grads_all[:, :query_cols]
+    grad_key = grads_all[:, query_cols : query_cols + key_value_columns]
+    grad_value = grads_all[:, query_cols + key_value_columns :]
+    return (grad_tokens, grad_query, grad_key, grad_value)
 
 
 def solution(mesh):
-    in_specs = (
-        P("dp", None),
-        P("dp", "tensor"),
-        P("dp", "tensor"),
-        P("dp", "tensor"),
-        P("dp", "tensor"),
-    )
-    out_specs = (P("dp", "tensor"), P("dp", "tensor"), P("dp", "tensor"), P("dp", "tensor"))
-    return jax.shard_map(body, mesh=mesh, in_specs=in_specs, out_specs=out_specs, check_vma=False)
+    view = Mesh(mesh.devices.reshape(4, 2, 4, 2, 2), DP_AXES + TP_AXES)
+    rows = P(DP_AXES, None)
+    split = P(DP_AXES, TP_AXES)
+    in_specs = (rows, split, split, split, split)
+    out_specs = (split, split, split, split)
+    return jax.shard_map(body, mesh=view, in_specs=in_specs, out_specs=out_specs, check_vma=False)

time: 890 us -> 409 us (0.46)
  waiting for transfers between devices: 742 us -> 283 us
  matrix products: 91.3 us -> 60.9 us
  blocking collectives: 0 us -> 14.5 us
    all_gather x3 -> x2, waiting for transfers between devices: 428 us -> 97.1 us  [the longest x1 64.7 us: gather_rows(): return lax.all_gather(block, 'y', axis=0, tiled=True)]
    reduce_scatter x0 -> x3, waiting for transfers between devices: none -> 174 us  [the longest x1 78.9 us: body(): lax.psum_scatter(partial_sum.astype(jnp.bfloat16), TP_AXES, scatter_dimen...]
    unnamed x6 -> x7, waiting for transfers between devices: 175 us -> 11.7 us
    psum x1 -> x0, waiting for transfers between devices: 139 us -> none  [body(): lax.psum(partial_sum.astype(jnp.bfloat16), 'tensor').astype(jnp.float32)]
    dot_general x5 -> x2, matrix products: 46.3 us -> 22.8 us  [the longest x1 11.8 us: body(): lax.dot_general(combined, weights_all, (((1,), (1,)), ((), ())), preferre...]
    all_gather x0 -> x1, blocking collectives: none -> 14.5 us  [gather_rows(): block = lax.all_gather(block, 'x', axis=0, tiled=True)]
  transfers between devices with their start and end apart: 5 -> 6, of which waited for: 5 -> 6; matrix products, arithmetic and copies ran while one was open for 7% -> 5% of each run, Pallas kernels for 0% -> 0%
where the time goes in v1:
time: 409 us; the launch traced here: 408 us
  waiting for transfers between devices  283 us (69%)
  matrix products  60.9 us (15%)
  other arithmetic  21.5 us (5%)
  blocking collectives  14.5 us (4%)
  between operations  14.4 us (4%)
  local copies, waits for them, and re-layouts  13.7 us (3%)
    reduce_scatter x1, waiting for transfers between devices, body(): lax.psum_scatter(partial_sum.astype(jnp.bfloat16), TP_AXES, scatter_dimen...  78.9 us
    all_gather x1, waiting for transfers between devices, gather_rows(): return lax.all_gather(block, 'y', axis=0, tiled=True)  64.7 us
    reduce_scatter x1, waiting for transfers between devices, scatter_rows(): block = lax.psum_scatter(block, 'y', scatter_dimension=0, tiled=True)  64.7 us
    all_gather x1, waiting for transfers between devices, gather_rows(): block = lax.all_gather(block, 'zl', axis=0, tiled=True)  32.4 us
    reduce_scatter x1, waiting for transfers between devices, scatter_rows(): block = lax.psum_scatter(block, 'zl', scatter_dimension=0, tiled=True)  30.5 us
    all_gather x1, blocking collectives, gather_rows(): block = lax.all_gather(block, 'x', axis=0, tiled=True)  14.5 us
    dot_general x1, matrix products, body(): lax.dot_general(combined, weights_all, (((1,), (1,)), ((), ())), preferre...  11.8 us
    unnamed x7, waiting for transfers between devices  11.7 us
  transfers between devices with their start and end apart: 6, of which 6 were waited for; matrix products, arithmetic and copies ran while one was open for 5% of the time, Pallas kernels for 0%

profile of v1, /device:TPU:0, one launch (start us, length us, event | category | flops | bytes accessed | tf_op | source)
XLA Modules:
  0.0 408.2 jit_solution(8105089729358219273)
XLA Ops:
  7.2 0.0 all-gather.3.cloned.1.call-start
  7.2 1.0 pad_maximum_fusion.6
  8.2 14.5 %all_gather.9 = bf16[512,768]{1,0:T(8,128)(2,1)} all-gather(bf16[128,768]{1,0:T(8,128)(2,1)S(1)} %pad_maximum_fusion.6), channel_id=1, replica_groups=mesh['y'=4,'zl'=2,'x'=4,'zh'=2,'c'=2] {'x'}, dimensions={0}, use_global_device_ids=true | all-gather | bytes 983040 | tf_op jit(solution)/shard_map/all_gather | solution.py:91
  22.7 0.0 all-gather.3.cloned.1.call-update
  22.7 0.0 all-gather.5.cloned.1.call-start
  22.7 32.4 %all-gather.3.cloned.1.call-done = bf16[1024,768]{1,0:T(8,128)(2,1)} async-done(((bf16[512,768]{1,0:T(8,128)(2,1)}), bf16[1024,768]{1,0:T(8,128)(2,1)}) %all-gather.3.cloned.1.call-update) | async-done | bytes 1572880 | tf_op jit(solution)/shard_map/all_gather | solution.py:92
  55.1 0.0 all-gather.5.cloned.1.call-update
  55.1 0.0 reduce-scatter.9.cloned.1.call-start
  55.2 2.3 copy.44
  57.5 0.3 iota_compare_fusion
  57.8 1.0 fusion.34
  58.8 64.7 %all-gather.5.cloned.1.call-done = bf16[4096,768]{1,0:T(8,128)(2,1)} async-done(((bf16[1024,768]{1,0:T(8,128)(2,1)}), bf16[4096,768]{1,0:T(8,128)(2,1)}) %all-gather.5.cloned.1.call-update) | async-done | bytes 6291472 | tf_op jit(solution)/shard_map/all_gather | solution.py:93
  123.5 11.0 %convolution_bitcast_fusion = f32[1024,768]{0,1:T(8,128)S(1)} fusion(bf16[4096,768]{1,0:T(8,128)(2,1)} %all-gather.5.cloned.1.call-done, bf16[1024,4096]{1,0:T(8,128)(2,1)} %param.5), kind=kOutput, calls=%fused_computation.29 | convolution fusion | flops 6442450944 | bytes 17825792 | tf_op jit(solution)/shard_map/dot_general | solution.py:107
  134.6 1.6 slice.26
  136.2 1.8 slice_negate_fusion.1
  138.0 0.2 pad_maximum_fusion.4
  138.2 0.3 maximum_multiply_fusion
  138.5 0.5 copy-done.5
  139.0 0.6 fusion.14
  139.5 0.7 copy-done.1
  140.3 3.1 fusion.6
  143.4 3.7 fusion.5
  147.1 0.6 copy-done.14
  147.7 6.0 %fusion.20 = bf16[1024,128]{0,1:T(8,128)(2,1)} fusion(bf16[1024,4,128]{0,2,1:T(8,128)(2,1)S(1)} %bitcast.123, f32[4,1024]{1,0:T(4,128)S(1)} %fusion.5, f32[4,1024]{1,0:T(4,128)S(1)} %get-tuple-element.27, f32[1024,1024,4]{1,0,2:T(8,128)S(1)} %get-tuple-element.28, pred[1024,1024]{0,1:T(8,128)(4,1)S(1)} %iota_compare_fusion), kind=kOutput, calls=%fused_computation.33 | convolution fusion | flops 1094844416 | bytes 19169280 | tf_op jit(solution)/shard_map/kgij,ikgd->jkd/dot_general | solution.py:71
  153.7 11.1 %fusion = (f32[4,1024]{1,0:T(4,128)}, f32[1024,1024,4]{1,0,2:T(8,128)}) fusion(f32[4,1024]{1,0:T(4,128)} %copy-done.14, f32[4,1024]{1,0:T(4,128)} %copy-done.13, f32[1024,1024,4]{1,0,2:T(8,128)S(1)} %get-tuple-element.28, pred[1024,1024]{0,1:T(8,128)(4,1)S(1)} %iota_compare_fusion, bf16[1024,4,128]{0,2,1:T(8,128)(2,1)} %bitcast.122, f32[1024,768]{0,1:T(8,128)} %copy-done.2), kind=kOutput, calls=%fused_computation.3 | convolution fusion | flops 1098903552 | bytes 35962880 | tf_op jit(solution)/shard_map/ikgd,jkd->kgij/dot_general | solution.py:64
  164.8 11.6 %fusion.7 = bf16[4,1024,1024]{1,2,0:T(8,128)(2,1)} fusion(f32[1024,1024,4]{1,0,2:T(8,128)} %get-tuple-element.30, f32[4,1024]{1,0:T(4,128)} %get-tuple-element.29, f32[4,1024]{1,0:T(4,128)} %copy-done.14, f32[4,1024]{1,0:T(4,128)} %copy-done.13, f32[1024,1024,4]{1,0,2:T(8,128)S(1)} %get-tuple-element.28, pred[1024,1024]{0,1:T(8,128)(4,1)S(1)} %iota_compare_fusion), kind=kLoop, calls=%fused_computation.11 | loop fusion | flops 33554432 | bytes 43040768 | tf_op jit(solution)/shard_map/reshape.19
  176.4 7.8 %bitcast_multiply_fusion.4 = (f32[1024,1,128]{0,2,1:T(8,128)S(1)}, f32[1024,1,128]{0,2,1:T(8,128)S(1)}) fusion(f32[1024,64]{0,1:T(8,128)} %copy-done.7, bf16[4,1024,1024]{1,2,0:T(8,128)(2,1)} %fusion.7, f32[1024,4,128]{0,2,1:T(8,128)} %copy-done.1, f32[1024,4,128]{0,2,1:T(8,128)} %bitcast.7, f32[1024,128]{0,1:T(8,128)} %copy-done.3), kind=kOutput, calls=%fused_computation.45 | convolution fusion | flops 1075576832 | bytes 14417920 | tf_op jit(solution)/shard_map/kgij,ikgd->jkd/dot_general | solution.py:70
  184.3 1.4 bitcast_multiply_fusion.3
  185.7 0.2 slice_negate_fusion
  185.9 0.2 pad_maximum_fusion
  186.2 0.5 copy-done.4
  186.7 0.6 fusion.16
  187.3 0.1 fusion.27
  187.4 0.7 slice-done
  188.1 0.0 copy-done.15
  188.2 1.3 slice-done.1
  189.5 8.7 %fusion.11 = bf16[4096,768]{0,1:T(8,128)(2,1)} fusion(bf16[1024,4096]{1,0:T(8,128)(2,1)S(1)} %bitcast.125, bf16[1024,128]{0,1:T(8,128)(2,1)S(1)} %copy-done.15, bf16[1024,128]{0,1:T(8,128)(2,1)S(1)} %fusion.27, bf16[1024,512]{0,1:T(8,128)(2,1)S(1)} %fusion.16), kind=kOutput, calls=%fused_computation.17 | convolution fusion | flops 6450315264 | bytes 16252928 | tf_op jit(solution)/shard_map/dot_general | solution.py:122
  198.2 0.0 reduce-scatter.11.cloned.1.call-start
  198.2 64.7 %reduce-scatter.9.cloned.1.call-done = bf16[1024,768]{0,1:T(8,128)(2,1)} async-done(((bf16[4096,768]{0,1:T(8,128)(2,1)}), bf16[1024,768]{0,1:T(8,128)(2,1)}) %reduce-scatter.9.cloned.1.call-update) | async-done | bytes 1572880 | tf_op jit(solution)/shard_map/reduce_scatter | solution.py:97
  263.0 0.0 reduce-scatter.13.cloned.1.call-start
  263.0 30.5 %reduce-scatter.11.cloned.1.call-done = bf16[512,768]{0,1:T(8,128)(2,1)} async-done(((bf16[1024,768]{0,1:T(8,128)(2,1)}), bf16[512,768]{0,1:T(8,128)(2,1)}) %reduce-scatter.11.cloned.1.call-update) | async-done | bytes 786448 | tf_op jit(solution)/shard_map/reduce_scatter | solution.py:98
  293.6 2.4 copy.39
  296.0 0.0 reduce-scatter.7.cloned.1.call-start
  296.0 11.8 %convolution_convert_fusion = bf16[1024,4096]{1,0:T(8,128)(2,1)} fusion(bf16[4096,768]{1,0:T(8,128)(2,1)} %all-gather.5.cloned.1.call-done, bf16[1024,128]{0,1:T(8,128)(2,1)S(1)} %copy-done.15, bf16[1024,128]{0,1:T(8,128)(2,1)S(1)} %fusion.27, bf16[1024,512]{0,1:T(8,128)(2,1)S(1)} %fusion.16), kind=kOutput, calls=%fused_computation.15 | convolution fusion | flops 6451363840 | bytes 16252928 | tf_op jit(solution)/shard_map/dot_general | solution.py:115
  307.9 11.6 %reduce-scatter.13.cloned.1.call-done = bf16[128,768]{1,0:T(8,128)(2,1)} async-done(((bf16[512,768]{1,0:T(8,128)(2,1)}), bf16[128,768]{1,0:T(8,128)(2,1)}) %reduce-scatter.13.cloned.1.call-update) | async-done | bytes 196624
  319.5 1.6 slice.28
  321.0 1.4 fusion.39
  322.5 78.9 %reduce-scatter.7.cloned.1.call-done = bf16[1024,1024]{1,0:T(8,128)(2,1)} async-done(((bf16[1024,4096]{1,0:T(8,128)(2,1)}), bf16[1024,1024]{1,0:T(8,128)(2,1)}) %reduce-scatter.7.cloned.1.call-update) | async-done | bytes 2097168 | tf_op jit(solution)/shard_map/reduce_scatter | solution.py:118
  (38 shorter events, 0.3 us)
Async XLA Ops:
  7.2 48.0 %all-gather.3.cloned.1.call-start = ((), (), s32[]{:S(2)}) async-start(), calls=%async_computation.4 | async-start | bytes 2359296 | tf_op jit(solution)/shard_map/all_gather | solution.py:92
  22.7 100.8 %all-gather.5.cloned.1.call-start = ((), (), s32[]{:S(2)}) async-start(), calls=%async_computation.5 | async-start | bytes 7864320 | tf_op jit(solution)/shard_map/all_gather | solution.py:93
  55.1 207.8 %reduce-scatter.9.cloned.1.call-start = ((), (), s32[]{:S(2)}) async-start(), calls=%async_computation.7 | async-start | bytes 7864320 | tf_op jit(solution)/shard_map/reduce_scatter | solution.py:97
  58.8 79.2 %copy-start.7 = (f32[1024,64]{0,1:T(8,128)}, f32[1024,64]{0,1:T(8,128)S(1)}, u32[]{:S(2)}) copy-start(f32[1024,64]{0,1:T(8,128)S(1)} %get-tuple-element.26) | copy-start | bytes 786436
  58.8 79.2 %copy-start.10 = (f32[1024,64]{0,1:T(8,128)}, f32[1024,64]{0,1:T(8,128)S(1)}, u32[]{:S(2)}) copy-start(f32[1024,64]{0,1:T(8,128)S(1)} %get-tuple-element.25) | copy-start | bytes 786436
  134.5 4.4 %copy-start.2 = (f32[1024,768]{0,1:T(8,128)}, f32[1024,768]{0,1:T(8,128)S(1)}, u32[]{:S(2)}) copy-start(f32[1024,768]{0,1:T(8,128)S(1)} %convolution_bitcast_fusion) | copy-start | bytes 9437188
  138.2 0.8 copy-start.5
  138.2 1.4 copy-start.3
  138.2 5.2 %copy-start.8 = (bf16[1024,128,1]{0,1,2:T(8,128)(2,1)}, bf16[1024,128,1]{0,1,2:T(8,128)(2,1)S(1)}, u32[]{:S(2)}) copy-start(bf16[1024,128,1]{0,1,2:T(8,128)(2,1)S(1)} %get-tuple-element.21) | copy-start | bytes 786436
  139.0 1.3 copy-start.1
  143.4 3.7 copy-start.13
  143.4 4.3 %copy-start.12 = (bf16[1024,512]{0,1:T(8,128)(2,1)S(1)}, bf16[1024,512]{0,1:T(8,128)(2,1)}, u32[]{:S(2)}) copy-start(bf16[1024,512]{0,1:T(8,128)(2,1)} %copy.44) | copy-start | bytes 3145732
  147.1 0.6 copy-start.14
  176.4 7.9 %copy-start = (bf16[4,1024,1024]{1,2,0:T(8,128)(2,1)S(1)}, bf16[4,1024,1024]{1,2,0:T(8,128)(2,1)}, u32[]{:S(2)}) copy-start(bf16[4,1024,1024]{1,2,0:T(8,128)(2,1)} %fusion.7) | copy-start | bytes 25165828
  176.4 7.9 %copy-start.6 = (f32[1024,128]{0,1:T(8,128)S(1)}, f32[1024,128]{0,1:T(8,128)}, u32[]{:S(2)}) copy-start(f32[1024,128]{0,1:T(8,128)} %copy-done.5) | copy-start | bytes 1572868
  176.4 7.9 %copy-start.9 = (bf16[1024,128,1]{0,1,2:T(8,128)(2,1)S(1)}, bf16[1024,128,1]{0,1,2:T(8,128)(2,1)}, u32[]{:S(2)}) copy-start(bf16[1024,128,1]{0,1,2:T(8,128)(2,1)} %copy-done.8) | copy-start | bytes 786436
  185.7 1.0 copy-start.4
  185.7 1.6 copy-start.11
  185.7 2.4 slice-start
  185.9 2.3 copy-start.15
  185.9 3.6 slice-start.1
  198.2 95.4 %reduce-scatter.11.cloned.1.call-start = ((), (), s32[]{:S(2)}) async-start(), calls=%async_computation.8 | async-start | bytes 2359296 | tf_op jit(solution)/shard_map/reduce_scatter | solution.py:98
  263.0 56.5 %reduce-scatter.13.cloned.1.call-start = ((), (), s32[]{:S(2)}) async-start(), calls=%async_computation.9 | async-start | bytes 983040
  296.0 105.4 %reduce-scatter.7.cloned.1.call-start = ((), (), s32[]{:S(2)}) async-start(), calls=%async_computation.6 | async-start | bytes 10485760 | tf_op jit(solution)/shard_map/reduce_scatter | solution.py:118
Sparse Core Ops, SparseCore 0:
  22.8 32.2 all-gather.2
  56.8 66.6 all-gather.4
  198.3 64.5 reduce-scatter.8
  265.2 28.3 reduce-scatter.10
  296.1 23.3 reduce-scatter.12
  322.8 78.5 reduce-scatter.6
